TPU v7x, 32 devices: a whole 2x2x4 slice. The times are simulated.
32 devices in a mesh: ctx: 8 (over z, y), tp: 4 (over x, core).
Axes of the slice: x: 2, y: 2, z: 4, core: 2. Of those that a mesh axis runs over, the one named last changes fastest.
Arguments:
- features: bfloat16 [2048, 8192], P('ctx', 'tp'), may hold values from -6 to 6
- input_map: bfloat16 [2048, 512], P('ctx', 'tp'), may hold values from -1.5 to 1.5
- output_map: bfloat16 [2048, 512], P('ctx', 'tp'), may hold values from -1.5 to 1.5
- gate_in: bfloat16 [2048, 8192], P('ctx', 'tp'), may hold values from -6 to 6
- conv_feat: float32 [4, 8192], P(None, 'tp'), may hold values from -3 to 3
- conv_input: float32 [4, 512], P(None, 'tp'), may hold values from -3 to 3
- conv_output: float32 [4, 512], P(None, 'tp'), may hold values from -3 to 3
- step_size: float32 [2048, 128], P('ctx', 'tp'), may hold values from 0.1 to 1
- log_decay: float32 [2048, 128], P('ctx', 'tp'), may hold values from -1 to 0, as said below
- skip_gain: float32 [128], P('tp'), may hold values from 0.5 to 2
- norm_gain: float32 [8192], P('tp'), may hold values from 0.5 to 1.5
- out_weight: bfloat16 [8192, 4096], P('tp', 'ctx'), may hold values from -0.0625 to 0.0625
Outputs:
- layer_out: bfloat16 [2048, 4096], P('ctx', 'tp')
Inputs may be any that keep to these rules, and one draw needn't show every extreme that they name: log_decay is negative.
All inputs are finite; a program needn't handle non-finite values.
Results may differ from a plain program's by a relative error of at most 0.0066.
Values may be sent and summed in bfloat16 or wider, within the bound.
No kernel may reach another device: no remote copies, remote signals or barrier semaphores. Data moves between devices by JAX's collectives and lax.ppermute only.
A program may use at most 192 MiB of HBM per device.

v0:
```python
import jax
import jax.numpy as jnp
from jax import lax
from jax.sharding import PartitionSpec as P

N = 128
BLOCK = 256


def shifted(value, axis, steps):
    count = lax.axis_size(axis)
    first, last = (max(0, -steps), min(count, count - steps))
    return lax.ppermute(value, axis, [(source, source + steps) for source in range(first, last)])


def local_conv(packed, kernel, tok_rows):
    tail_len = kernel.shape[0] - 1
    padded = jnp.pad(packed.astype(jnp.float32), ((tail_len, 0), (0, 0)))
    pre_act = jnp.zeros((tok_rows, kernel.shape[1]), jnp.float32)
    for tap_index in range(kernel.shape[0]):
        pre_act = pre_act + kernel[tap_index] * padded[tap_index : tap_index + tok_rows]
    return pre_act


def edge_partial(tail_rows, kernel):
    tail_len = kernel.shape[0] - 1
    tail_vals = tail_rows.astype(jnp.float32)
    outputs = []
    for row_index in range(tail_len):
        accum = jnp.zeros((kernel.shape[1],), jnp.float32)
        for tap_index in range(tail_len - row_index):
            accum = accum + kernel[tap_index] * tail_vals[row_index + tap_index]
        outputs.append(accum)
    return jnp.stack(outputs, axis=0)


def intra_block(scaled, b_rows, c_rows, cum_log):
    scores = jnp.einsum("tgn,sgn->gts", c_rows, b_rows, preferred_element_type=jnp.float32)
    cum_cols = jnp.moveaxis(cum_log, 0, -1)
    log_gap = cum_cols[..., :, None] - cum_cols[..., None, :]
    block_len = cum_log.shape[0]
    causal = jnp.arange(block_len)[:, None] >= jnp.arange(block_len)[None, :]
    decays = jnp.exp(jnp.where(causal, log_gap, -jnp.inf))
    weights = (scores[:, None] * decays).astype(jnp.bfloat16)
    return jnp.einsum("gjts,sgjp->tgjp", weights, scaled, preferred_element_type=jnp.float32)


def block_state(scaled, b_rows, cum_log):
    end_decay = jnp.exp(cum_log[-1][None] - cum_log)
    b_weighted = (b_rows.astype(jnp.float32)[:, :, None, :] * end_decay[..., None]).astype(
        jnp.bfloat16
    )
    return jnp.einsum("sgjp,sgjn->gjpn", scaled, b_weighted, preferred_element_type=jnp.float32)


def inter_block(c_rows, cum_log, state_carry):
    rounded = state_carry.astype(jnp.bfloat16)
    inner = jnp.einsum("tgn,gjpn->tgjp", c_rows, rounded, preferred_element_type=jnp.float32)
    return inner * jnp.exp(cum_log)[..., None]


def combine(first_part, second_part):
    decay_first, state_first = first_part
    decay_second, state_second = second_part
    return (decay_first * decay_second, decay_second[..., None, None] * state_first + state_second)


def prefix_states(dev_decay, dev_state):
    count = lax.axis_size("ctx")
    own = (dev_decay, dev_state)
    if count == 1:
        return jnp.zeros_like(dev_state)
    got = shifted(own, "ctx", 1)
    before = got
    upto = combine(got, own)
    step = 2
    while step < count:
        got = shifted(upto, "ctx", step)
        before = combine(got, before)
        if step * 2 < count:
            upto = combine(got, upto)
        step *= 2
    return before[1]


def on_device(
    features,
    input_map,
    output_map,
    gate_in,
    conv_feat,
    conv_input,
    conv_output,
    step_size,
    log_decay,
    skip_gain,
    norm_gain,
    out_weight,
):
    tok_rows, width_x = features.shape
    width_b = input_map.shape[1]
    head_count = step_size.shape[1]
    head_dim = width_x // head_count
    groups_here = width_b // N
    per_group = head_count // groups_here
    tail_len = conv_feat.shape[0] - 1
    n_blocks = tok_rows // BLOCK
    packed = jnp.concatenate([features, input_map, output_map], axis=1)
    kernel = jnp.concatenate([conv_feat, conv_input, conv_output], axis=1)
    pre_act = local_conv(packed, kernel, tok_rows)
    tail_rows = shifted(packed[tok_rows - tail_len :], "ctx", 1)
    edge_sums = edge_partial(tail_rows, kernel)
    pre_act = pre_act + jnp.pad(edge_sums, ((0, tok_rows - tail_len), (0, 0)))
    conv_out = jax.nn.silu(pre_act).astype(jnp.bfloat16)
    x_conv = conv_out[:, :width_x]
    b_conv = conv_out[:, width_x : width_x + width_b]
    c_conv = conv_out[:, width_x + width_b :]
    x_heads = x_conv.astype(jnp.float32).reshape(tok_rows, groups_here, per_group, head_dim)
    scaled = (x_heads * step_size.reshape(tok_rows, groups_here, per_group)[..., None]).astype(
        jnp.bfloat16
    )

    def blocked(value_entries):
        return value_entries.reshape((n_blocks, BLOCK) + value_entries.shape[1:])

    scaled_b = blocked(scaled)
    b_rows = blocked(b_conv.reshape(tok_rows, groups_here, N))
    c_rows = blocked(c_conv.reshape(tok_rows, groups_here, N))
    cum_log = jnp.cumsum(blocked(log_decay.reshape(tok_rows, groups_here, per_group)), axis=1)
    blk_states = jax.vmap(block_state)(scaled_b, b_rows, cum_log)
    blk_decay = jnp.exp(cum_log[:, -1])

    def fold_local(state_carry, block_in):
        decay_b, state_b = block_in
        return (decay_b[..., None, None] * state_carry + state_b, None)

    dev_state, _ = lax.scan(
        fold_local, jnp.zeros(blk_states.shape[1:], jnp.float32), (blk_decay, blk_states)
    )
    dev_decay = jnp.prod(blk_decay, axis=0)
    incoming = prefix_states(dev_decay, dev_state)

    def advance(state_carry, block_in):
        scaled_k, b_k, c_k, cum_k, decay_k, state_k = block_in
        block_y = intra_block(scaled_k, b_k, c_k, cum_k) + inter_block(c_k, cum_k, state_carry)
        return (decay_k[..., None, None] * state_carry + state_k, block_y)

    _, ssm_y = lax.scan(
        advance, incoming, (scaled_b, b_rows, c_rows, cum_log, blk_decay, blk_states)
    )
    mixed_y = ssm_y.reshape(tok_rows, groups_here, per_group, head_dim)
    mixed_y = mixed_y + skip_gain.reshape(groups_here, per_group)[..., None] * x_heads
    gated_y = mixed_y.reshape(tok_rows, width_x) * jax.nn.silu(gate_in.astype(jnp.float32))
    grouped = gated_y.reshape(tok_rows, groups_here, width_x // groups_here)
    inv_root = lax.rsqrt(jnp.mean(grouped * grouped, axis=-1, keepdims=True) + 1e-05)
    hidden = ((grouped * inv_root).reshape(tok_rows, width_x) * norm_gain).astype(jnp.bfloat16)
    partial_out = jnp.dot(
        hidden,
        lax.all_gather(out_weight, "ctx", axis=1, tiled=True),
        preferred_element_type=jnp.float32,
    )
    return lax.psum_scatter(partial_out, "tp", scatter_dimension=1, tiled=True).astype(jnp.bfloat16)


def solution(mesh):
    placed = (
        P("ctx", "tp"),
        P("ctx", "tp"),
        P("ctx", "tp"),
        P("ctx", "tp"),
        P(None, "tp"),
        P(None, "tp"),
        P(None, "tp"),
        P("ctx", "tp"),
        P("ctx", "tp"),
        P("tp"),
        P("tp"),
        P("tp", "ctx"),
    )
    return jax.shard_map(
        on_device, mesh=mesh, in_specs=placed, out_specs=P("ctx", "tp"), check_vma=False
    )
```

profile of v0, /device:TPU:0, one launch (start us, length us, event | category | flops | bytes accessed | tf_op | source)
XLA Modules:
  0.0 388.2 jit_solution(2838211451355489667)
XLA Ops:
  6.6 0.0 all-gather.2.cloned.1.call-start
  6.6 0.7 all-gather.2.cloned.1.call-update
  7.3 0.0 reduce-scatter.2.cloned.1.call-start
  7.3 0.4 copy-done.1
  7.8 0.1 constant_dynamic-update-slice_fusion.5
  7.9 0.0 copy-done.4
  7.9 4.9 %collective-permute-start = (bf16[3,2304]{1,0:T(4,128)(2,1)S(1)}, bf16[3,2304]{1,0:T(4,128)(2,1)S(1)}, u32[]{:S(2)}, u32[]{:S(2)}) collective-permute-start(bf16[3,2304]{1,0:T(4,128)(2,1)S(1)} %slice.83), channel_id=1, source_target_pairs={{0,4},{4,8},{8,12},{12,16},{16,20},{20,24},{24,28},{1,5},{5,9},{9,... | collective-permute-start | bytes 41480 | tf_op jit(solution)/shard_map/ppermute | solution.py:13
  12.9 0.6 reduce-window.6
  13.5 0.2 slice_reduce_fusion
  13.7 0.1 copy.30
  13.8 0.0 copy-done.7
  13.8 0.1 broadcast.89
  13.9 0.1 fusion.35
  14.0 0.6 exponential_reduce_fusion
  14.6 0.1 subtract_exponential_fusion
  14.7 0.0 copy-done.8
  14.7 0.2 convert_element_type.56
  14.9 0.0 collective-permute-done
  14.9 0.1 slice_reduce_fusion.5
  15.0 1.5 multiply_convert_fusion.3
  16.6 1.6 slice_convert_fusion
  18.2 2.3 copy.27
  20.5 1.4 fusion.18
  21.9 3.6 collective-permute-start.3
  25.5 41.7 %collective-permute-done.3 = f32[1,32,64,128]{3,2,1,0:T(8,128)S(1)} collective-permute-done((f32[1,32,64,128]{3,2,1,0:T(8,128)S(1)}, f32[1,32,64,128]{3,2,1,0:T(8,128)S(1)}, u32[]{:S(2)}, u32[]{:S(2)}) %collective-permute-start.3) | collective-permute-done | bytes 1048608 | tf_op jit(solution)/shard_map/ppermute | solution.py:13
  67.2 0.2 multiply_add_fusion.1
  67.5 8.8 %collective-permute-start.4 = (f32[1,32,64,128]{3,2,1,0:T(8,128)S(1)}, f32[1,32,64,128]{3,2,1,0:T(8,128)S(1)}, u32[]{:S(2)}, u32[]{:S(2)}) collective-permute-start(f32[1,32,64,128]{3,2,1,0:T(8,128)S(1)} %multiply_add_fusion.1), channel_id=1, source_target_pairs={{0,8},{4,12},{8,16},{12,20},{16,24},{20,28},{1,9},{5,13},{9,17},{1... | collective-permute-start | bytes 3145736 | tf_op jit(solution)/shard_map/ppermute | solution.py:13
  76.3 11.8 %collective-permute-start.1 = (f32[1,32]{1,0:T(1,128)S(1)}, f32[1,32]{1,0:T(1,128)S(1)}, u32[]{:S(2)}, u32[]{:S(2)}) collective-permute-start(f32[1,32]{1,0:T(1,128)S(1)} %bitcast.73), channel_id=1, source_target_pairs={{0,4},{4,8},{8,12},{12,16},{16,20},{20,24},{24,28},{1,5},{5,9},{9,... | collective-permute-start | bytes 392 | tf_op jit(solution)/shard_map/ppermute | solution.py:13
  88.2 1.2 collective-permute-done.1
  89.4 7.1 %collective-permute-done.4 = f32[1,32,64,128]{3,2,1,0:T(8,128)S(1)} collective-permute-done((f32[1,32,64,128]{3,2,1,0:T(8,128)S(1)}, f32[1,32,64,128]{3,2,1,0:T(8,128)S(1)}, u32[]{:S(2)}, u32[]{:S(2)}) %collective-permute-start.4) | collective-permute-done | bytes 1048608 | tf_op jit(solution)/shard_map/ppermute | solution.py:13
  96.5 0.2 multiply_add_fusion
  96.7 45.2 %collective-permute-start.5 = (f32[1,32,64,128]{3,2,1,0:T(8,128)S(1)}, f32[1,32,64,128]{3,2,1,0:T(8,128)S(1)}, u32[]{:S(2)}, u32[]{:S(2)}) collective-permute-start(f32[1,32,64,128]{3,2,1,0:T(8,128)S(1)} %multiply_add_fusion), channel_id=1, source_target_pairs={{0,16},{4,20},{8,24},{12,28},{1,17},{5,21},{9,25},{13,29},{2,18},{... | collective-permute-start | bytes 3145736 | tf_op jit(solution)/shard_map/ppermute | solution.py:13
  141.9 3.4 collective-permute-start.2
  145.3 41.9 %collective-permute-done.2 = f32[1,32]{1,0:T(1,128)S(1)} collective-permute-done((f32[1,32]{1,0:T(1,128)S(1)}, f32[1,32]{1,0:T(1,128)S(1)}, u32[]{:S(2)}, u32[]{:S(2)}) %collective-permute-start.2) | collective-permute-done | bytes 160 | tf_op jit(solution)/shard_map/ppermute | solution.py:13
  187.2 0.2 fusion.27
  187.4 0.0 copy-start.9
  187.4 2.1 fusion
  189.5 0.0 collective-permute-done.5
  189.5 2.1 fusion.14
  191.6 2.0 copy.32
  193.6 0.0 copy-done.2
  193.6 0.0 copy-start.10
  193.6 0.8 multiply_reduce_fusion
  194.4 132.1 %all-gather.2.cloned.1.call-done = bf16[2048,4096]{1,0:T(8,128)(2,1)} async-done(((bf16[2048,512]{1,0:T(8,128)(2,1)}), bf16[2048,4096]{1,0:T(8,128)(2,1)}) %all-gather.2.cloned.1.call-update) | async-done | bytes 16777232 | tf_op jit(solution)/shard_map/all_gather | solution.py:159
  326.5 10.5 %fusion.19 = f32[256,4096]{1,0:T(8,128)} fusion(bf16[2048,4096]{1,0:T(8,128)(2,1)} %all-gather.2.cloned.1.call-done, f32[2048]{0:T(1024)S(1)} %copy-done.10, f32[256]{0:T(256)S(1)} %add_rsqrt_fusion, f32[256,2048]{1,0:T(8,128)S(1)} %copy.32, bf16[256,2048]{1,0:T(8,128)(2,1)S(1)} %copy-done.2), kind=kOutput, calls=%fused_computation.32 | convolution fusion | flops 4299685888 | bytes 24126464 | tf_op jit(solution)/shard_map/dot_general | solution.py:157
  337.1 0.0 reduce-scatter.2.cloned.1.call-update
  337.1 42.2 %reduce-scatter.2.cloned.1.call-done = f32[256,1024]{1,0:T(8,128)} async-done(((f32[256,4096]{1,0:T(8,128)}), f32[256,1024]{1,0:T(8,128)}) %reduce-scatter.2.cloned.1.call-update) | async-done | bytes 1048592 | tf_op jit(solution)/shard_map/reduce_scatter | solution.py:162
  379.3 2.1 convert_element_type.67
  (36 shorter events, 0.3 us)
Async XLA Ops:
  6.5 6.3 %copy-start = (f32[256,32]{0,1:T(8,128)S(1)}, f32[256,32]{0,1:T(8,128)}, u32[]{:S(2)}) copy-start(f32[256,32]{0,1:T(8,128)} %param.20) | copy-start | bytes 98308
  6.5 1.2 copy-start.1
  6.5 1.3 copy-start.3
  6.5 1.3 copy-start.4
  6.5 7.3 %copy-start.6 = (f32[4,2048]{1,0:T(4,128)S(1)}, f32[4,2048]{1,0:T(4,128)}, u32[]{:S(2)}) copy-start(f32[4,2048]{1,0:T(4,128)} %param.16) | copy-start | bytes 98308
  6.5 7.3 %copy-start.7 = (f32[4,128]{1,0:T(4,128)S(1)}, f32[4,128]{1,0:T(4,128)}, u32[]{:S(2)}) copy-start(f32[4,128]{1,0:T(4,128)} %param.17) | copy-start | bytes 6148
  6.6 8.1 %copy-start.8 = (f32[4,128]{1,0:T(4,128)S(1)}, f32[4,128]{1,0:T(4,128)}, u32[]{:S(2)}) copy-start(f32[4,128]{1,0:T(4,128)} %param.18) | copy-start | bytes 6148
  6.6 319.9 %all-gather.2.cloned.1.call-start = ((), (), s32[]{:S(2)}) async-start(), calls=%async_computation.1 | async-start | bytes 18874368 | tf_op jit(solution)/shard_map/all_gather | solution.py:159
  7.3 372.0 %reduce-scatter.2.cloned.1.call-start = ((), (), s32[]{:S(2)}) async-start(), calls=%async_computation.2 | async-start | bytes 5242880 | tf_op jit(solution)/shard_map/reduce_scatter | solution.py:162
  7.9 6.9 %collective-permute-start = (bf16[3,2304]{1,0:T(4,128)(2,1)S(1)}, bf16[3,2304]{1,0:T(4,128)(2,1)S(1)}, u32[]{:S(2)}, u32[]{:S(2)}) collective-permute-start(bf16[3,2304]{1,0:T(4,128)(2,1)S(1)} %slice.83), channel_id=1, source_target_pairs={{0,4},{4,8},{8,12},{12,16},{16,20},{20,24},{24,28},{1,5},{5,9},{9,... | collective-permute-start | bytes 41480 | tf_op jit(solution)/shard_map/ppermute | solution.py:13
  18.2 2.3 copy-start.5
  21.9 45.3 %collective-permute-start.3 = (f32[1,32,64,128]{3,2,1,0:T(8,128)S(1)}, f32[1,32,64,128]{3,2,1,0:T(8,128)S(1)}, u32[]{:S(2)}, u32[]{:S(2)}) collective-permute-start(f32[1,32,64,128]{3,2,1,0:T(8,128)S(1)} %fusion.18), channel_id=1, source_target_pairs={{0,4},{4,8},{8,12},{12,16},{16,20},{20,24},{24,28},{1,5},{5,9},{9,... | collective-permute-start | bytes 3145736 | tf_op jit(solution)/shard_map/ppermute | solution.py:13
  67.5 29.0 %collective-permute-start.4 = (f32[1,32,64,128]{3,2,1,0:T(8,128)S(1)}, f32[1,32,64,128]{3,2,1,0:T(8,128)S(1)}, u32[]{:S(2)}, u32[]{:S(2)}) collective-permute-start(f32[1,32,64,128]{3,2,1,0:T(8,128)S(1)} %multiply_add_fusion.1), channel_id=1, source_target_pairs={{0,8},{4,12},{8,16},{12,20},{16,24},{20,28},{1,9},{5,13},{9,17},{1... | collective-permute-start | bytes 3145736 | tf_op jit(solution)/shard_map/ppermute | solution.py:13
  76.3 13.1 %collective-permute-start.1 = (f32[1,32]{1,0:T(1,128)S(1)}, f32[1,32]{1,0:T(1,128)S(1)}, u32[]{:S(2)}, u32[]{:S(2)}) collective-permute-start(f32[1,32]{1,0:T(1,128)S(1)} %bitcast.73), channel_id=1, source_target_pairs={{0,4},{4,8},{8,12},{12,16},{16,20},{20,24},{24,28},{1,5},{5,9},{9,... | collective-permute-start | bytes 392 | tf_op jit(solution)/shard_map/ppermute | solution.py:13
  96.7 92.8 %collective-permute-start.5 = (f32[1,32,64,128]{3,2,1,0:T(8,128)S(1)}, f32[1,32,64,128]{3,2,1,0:T(8,128)S(1)}, u32[]{:S(2)}, u32[]{:S(2)}) collective-permute-start(f32[1,32,64,128]{3,2,1,0:T(8,128)S(1)} %multiply_add_fusion), channel_id=1, source_target_pairs={{0,16},{4,20},{8,24},{12,28},{1,17},{5,21},{9,25},{13,29},{2,18},{... | collective-permute-start | bytes 3145736 | tf_op jit(solution)/shard_map/ppermute | solution.py:13
  141.9 45.3 %collective-permute-start.2 = (f32[1,32]{1,0:T(1,128)S(1)}, f32[1,32]{1,0:T(1,128)S(1)}, u32[]{:S(2)}, u32[]{:S(2)}) collective-permute-start(f32[1,32]{1,0:T(1,128)S(1)} %bitcast_multiply_fusion.1), channel_id=1, source_target_pairs={{0,8},{4,12},{8,16},{12,20},{16,24},{20,28},{1,9},{5,13},{9,17},{1... | collective-permute-start | bytes 392 | tf_op jit(solution)/shard_map/ppermute | solution.py:13
  187.4 2.1 copy-start.9
  191.6 2.0 copy-start.2
  193.6 132.9 %copy-start.10 = (f32[2048]{0:T(1024)S(1)}, f32[2048]{0:T(1024)}, u32[]{:S(2)}) copy-start(f32[2048]{0:T(1024)} %param.22) | copy-start | bytes 24580
Sparse Core Ops, SparseCore 0:
  9.4 317.0 all-gather.1
  337.2 42.0 reduce-scatter.1
where the time goes:
time: 389 us; the launch traced here: 388 us
  waiting for transfers between devices  267 us (69%)
  starting transfers between devices  77.8 us (20%)
  matrix products  16.3 us (4%)
  between operations  13.8 us (4%)
  other arithmetic  7.57 us (2%)
  local copies, waits for them, and re-layouts  5.83 us (1%)
    all_gather x1, waiting for transfers between devices, on_device(): lax.all_gather(out_weight, 'ctx', axis=1, tiled=True)  132 us
    ppermute x6, waiting for transfers between devices, shifted(): lax.ppermute(value, axis, [(source, source + steps) for source in range(f...  91.9 us
    ppermute x6, starting transfers between devices, shifted(): lax.ppermute(value, axis, [(source, source + steps) for source in range(f...  77.7 us
    reduce_scatter x1, waiting for transfers between devices, on_device(): lax.psum_scatter(partial_out, 'tp', scatter_dimension=1, tiled=True)  42.2 us
    dot_general x1, matrix products, on_device(): jnp.dot(hidden, lax.all_gather(out_weight, 'ctx', axis=1, tiled=True), pr...  10.5 us
  transfers between devices with their start and end apart: 8, of which 6 were waited for; matrix products, arithmetic and copies ran while one was open for 4% of the time, Pallas kernels for 0%

commit v1 on v0

--- a/solution.py
+++ b/solution.py
@@ -5,6 +5,22 @@
 
 N = 128
 BLOCK = 256
+
+
+def treat_the_strings(array_in, device_axis="ctx"):
+    k_now = lax.axis_size(device_axis)
+    piece_out = lax.axis_index(device_axis)
+    prior, r2 = (k_now, piece_out)
+    val2, raw_out = (array_in, 1)
+    while raw_out < prior:
+        row_out = lax.ppermute(
+            val2, axis_name=device_axis, perm=[(h, h ^ raw_out) for h in range(prior)]
+        )
+        met_up = jnp.concatenate([val2, row_out], axis=1)
+        wide_out = jnp.concatenate([row_out, val2], axis=1)
+        val2 = jnp.where(r2 & raw_out == 0, met_up, wide_out)
+        raw_out = 2 * raw_out
+    return val2
 
 
 def shifted(value, axis, steps):
@@ -154,11 +170,7 @@
     grouped = gated_y.reshape(tok_rows, groups_here, width_x // groups_here)
     inv_root = lax.rsqrt(jnp.mean(grouped * grouped, axis=-1, keepdims=True) + 1e-05)
     hidden = ((grouped * inv_root).reshape(tok_rows, width_x) * norm_gain).astype(jnp.bfloat16)
-    partial_out = jnp.dot(
-        hidden,
-        lax.all_gather(out_weight, "ctx", axis=1, tiled=True),
-        preferred_element_type=jnp.float32,
-    )
+    partial_out = jnp.dot(hidden, treat_the_strings(out_weight), preferred_element_type=jnp.float32)
     return lax.psum_scatter(partial_out, "tp", scatter_dimension=1, tiled=True).astype(jnp.bfloat16)
 
 

time: 389 us -> 708 us (1.82)
  starting transfers between devices: 77.8 us -> 397 us
  waiting for transfers between devices: 267 us -> 239 us
  other arithmetic: 7.57 us -> 26.3 us
  matrix products: 16.3 us -> 24.9 us
    ppermute x6, starting transfers between devices: 77.7 us -> 390 us  [shifted(): lax.ppermute(value, axis, [(source, source + steps) for source in range(f...]
    all_gather x1 -> x0, waiting for transfers between devices: 132 us -> none  [on_device(): lax.all_gather(out_weight, 'ctx', axis=1, tiled=True)]
    ppermute x0 -> x3, waiting for transfers between devices: none -> 132 us  [treat_the_strings(): lax.ppermute(val2, axis_name=device_axis, perm=[(h, h ^ raw_out) for h in...]
    ppermute x6, waiting for transfers between devices: 91.9 us -> 41.1 us  [shifted(): lax.ppermute(value, axis, [(source, source + steps) for source in range(f...]
    reduce_scatter x1, waiting for transfers between devices: 42.2 us -> 66.2 us  [on_device(): lax.psum_scatter(partial_out, 'tp', scatter_dimension=1, tiled=True)]
    select_n x0 -> x2, other arithmetic: none -> 16.2 us  [treat_the_strings(): val2 = jnp.where(r2 & raw_out == 0, met_up, wide_out)]
    dot_general x1, matrix products: 10.5 us -> 17.9 us  [on_device(): jnp.dot(hidden, treat_the_strings(out_weight), preferred_element_type=jnp...]
    ppermute x0 -> x3, starting transfers between devices: none -> 7.33 us  [treat_the_strings(): lax.ppermute(val2, axis_name=device_axis, perm=[(h, h ^ raw_out) for h in...]
  transfers between devices with their start and end apart: 8 -> 10, of which waited for: 6 -> 6; matrix products, arithmetic and copies ran while one was open for 4% -> 4% of each run, Pallas kernels for 0% -> 0%
where the time goes in v1:
time: 708 us; the launch traced here: 707 us
  starting transfers between devices  397 us (56%)
  waiting for transfers between devices  239 us (34%)
  other arithmetic  26.3 us (4%)
  matrix products  24.9 us (4%)
  between operations  13.8 us (2%)
    ppermute x6, starting transfers between devices, shifted(): lax.ppermute(value, axis, [(source, source + steps) for source in range(f...  390 us
    ppermute x3, waiting for transfers between devices, treat_the_strings(): lax.ppermute(val2, axis_name=device_axis, perm=[(h, h ^ raw_out) for h in...  132 us
    reduce_scatter x1, waiting for transfers between devices, on_device(): lax.psum_scatter(partial_out, 'tp', scatter_dimension=1, tiled=True)  66.2 us
    ppermute x6, waiting for transfers between devices, shifted(): lax.ppermute(value, axis, [(source, source + steps) for source in range(f...  41.1 us
    dot_general x1, matrix products, on_device(): jnp.dot(hidden, treat_the_strings(out_weight), preferred_element_type=jnp...  17.9 us
    select_n x2, other arithmetic, treat_the_strings(): val2 = jnp.where(r2 & raw_out == 0, met_up, wide_out)  16.2 us
  transfers between devices with their start and end apart: 10, of which 6 were waited for; matrix products, arithmetic and copies ran while one was open for 4% of the time, Pallas kernels for 0%

profile of v1, /device:TPU:0, one launch (start us, length us, event | category | flops | bytes accessed | tf_op | source)
XLA Modules:
  0.0 707.4 jit_solution(9496018099569232423)
XLA Ops:
  6.5 3.0 collective-permute-start.6
  9.5 45.8 %collective-permute-done.6 = bf16[2048,512]{1,0:T(8,128)(2,1)S(1)} collective-permute-done((bf16[2048,512]{1,0:T(8,128)(2,1)}, bf16[2048,512]{1,0:T(8,128)(2,1)S(1)}, u32[]{:S(2)}, u32[]{:S(2)}) %collective-permute-start.6) | collective-permute-done | bytes 2097184 | tf_op jit(solution)/shard_map/ppermute | solution.py:16
  55.4 4.9 maximum_select_fusion.3
  60.3 1.8 collective-permute-start.7
  62.1 0.1 constant_dynamic-update-slice_fusion.5
  62.3 3.4 collective-permute-start
  65.7 0.6 reduce-window.6
  66.3 0.2 slice_reduce_fusion
  66.5 0.0 copy-start.9
  66.6 0.0 copy-start.10
  66.6 85.8 %collective-permute-done.7 = bf16[2048,1024]{1,0:T(8,128)(2,1)} collective-permute-done((bf16[2048,1024]{1,0:T(8,128)(2,1)}, bf16[2048,1024]{1,0:T(8,128)(2,1)}, u32[]{:S(2)}, u32[]{:S(2)}) %collective-permute-start.7) | collective-permute-done | bytes 4194336 | tf_op jit(solution)/shard_map/ppermute | solution.py:16
  152.4 11.2 %maximum_select_fusion.2 = bf16[2048,2048]{1,0:T(8,128)(2,1)} fusion(bf16[2048,1024]{1,0:T(8,128)(2,1)} %collective-permute-done.7, bf16[2048,1024]{1,0:T(8,128)(2,1)} %maximum_select_fusion.3, pred[]{:T(512)S(6)} %eq.10), kind=kLoop, calls=%fused_computation.8 | loop fusion | flops 37748736 | bytes 16777216 | tf_op jit(solution)/shard_map/jit(_where)/select_n | solution.py:21
  163.6 2.5 collective-permute-start.8
  166.2 0.1 copy.30
  166.3 0.1 broadcast.89
  166.4 0.1 fusion.42
  166.5 0.5 exponential_reduce_fusion
  167.0 0.1 subtract_exponential_fusion
  167.2 0.2 convert_element_type.56
  167.3 0.0 collective-permute-done
  167.4 0.1 slice_reduce_fusion.5
  167.5 1.5 multiply_convert_fusion.3
  169.0 1.6 slice_convert_fusion
  170.6 1.9 copy.27
  172.6 1.4 fusion.25
  174.0 3.5 collective-permute-start.3
  177.5 20.3 %collective-permute-done.3 = f32[1,32,64,128]{3,2,1,0:T(8,128)S(1)} collective-permute-done((f32[1,32,64,128]{3,2,1,0:T(8,128)S(1)}, f32[1,32,64,128]{3,2,1,0:T(8,128)S(1)}, u32[]{:S(2)}, u32[]{:S(2)}) %collective-permute-start.3) | collective-permute-done | bytes 1048608 | tf_op jit(solution)/shard_map/ppermute | solution.py:29
  197.9 1.0 copy-done.1
  198.9 1.2 multiply_add_fusion.1
  200.1 175.3 %collective-permute-start.4 = (f32[1,32,64,128]{3,2,1,0:T(8,128)}, f32[1,32,64,128]{3,2,1,0:T(8,128)}, u32[]{:S(2)}, u32[]{:S(2)}) collective-permute-start(f32[1,32,64,128]{3,2,1,0:T(8,128)} %multiply_add_fusion.1), channel_id=1, source_target_pairs={{0,8},{4,12},{8,16},{12,20},{16,24},{20,28},{1,9},{5,13},{9,17},{1... | collective-permute-start | bytes 3145736 | tf_op jit(solution)/shard_map/ppermute | solution.py:29
  375.4 181.2 %collective-permute-start.1 = (f32[1,32]{1,0:T(1,128)S(1)}, f32[1,32]{1,0:T(1,128)S(1)}, u32[]{:S(2)}, u32[]{:S(2)}) collective-permute-start(f32[1,32]{1,0:T(1,128)S(1)} %bitcast.72), channel_id=1, source_target_pairs={{0,4},{4,8},{8,12},{12,16},{16,20},{20,24},{24,28},{1,5},{5,9},{9,... | collective-permute-start | bytes 392 | tf_op jit(solution)/shard_map/ppermute | solution.py:29
  556.6 1.2 collective-permute-done.1
  557.8 1.7 multiply_add_fusion
  559.6 24.5 %collective-permute-start.5 = (f32[1,32,64,128]{3,2,1,0:T(8,128)S(1)}, f32[1,32,64,128]{3,2,1,0:T(8,128)S(1)}, u32[]{:S(2)}, u32[]{:S(2)}) collective-permute-start(f32[1,32,64,128]{3,2,1,0:T(8,128)S(1)} %multiply_add_fusion), channel_id=1, source_target_pairs={{0,16},{4,20},{8,24},{12,28},{1,17},{5,21},{9,25},{13,29},{2,18},{... | collective-permute-start | bytes 3145736 | tf_op jit(solution)/shard_map/ppermute | solution.py:29
  584.1 2.2 collective-permute-start.2
  586.3 19.5 %collective-permute-done.2 = f32[1,32]{1,0:T(1,128)S(1)} collective-permute-done((f32[1,32]{1,0:T(1,128)S(1)}, f32[1,32]{1,0:T(1,128)S(1)}, u32[]{:S(2)}, u32[]{:S(2)}) %collective-permute-start.2) | collective-permute-done | bytes 160 | tf_op jit(solution)/shard_map/ppermute | solution.py:29
  605.8 0.2 fusion.33
  606.0 0.0 copy-start.11
  606.1 2.1 fusion.7
  608.2 0.0 collective-permute-done.5
  608.2 3.3 fusion.21
  611.5 2.0 copy.32
  613.5 0.0 copy-start.12
  613.5 0.8 multiply_reduce_fusion
  614.3 17.9 %fusion = f32[256,4096]{1,0:T(8,128)} fusion(bf16[2048,2048]{1,0:T(8,128)(2,1)} %collective-permute-done.8, bf16[2048,2048]{1,0:T(8,128)(2,1)} %maximum_select_fusion.2, pred[]{:T(512)S(6)} %eq.9, f32[2048]{0:T(1024)S(1)} %copy-done.12, f32[256]{0:T(256)S(1)} %add_rsqrt_fusion, f32[256,2048]{1,0:T(8,128)S(1)} %copy.32, bf16[256,2048]{1,0:T(8,128)(2,1)S(1)} %copy-done.4), kind=kOutput, calls=%fused_computation.1 | convolution fusion | flops 4375183360 | bytes 24126464 | tf_op jit(solution)/shard_map/dot_general | solution.py:173
  632.2 0.0 reduce-scatter.2.cloned.1.call-update
  632.3 66.2 %reduce-scatter.2.cloned.1.call-done = f32[256,1024]{1,0:T(8,128)} async-done(((f32[256,4096]{1,0:T(8,128)}), f32[256,1024]{1,0:T(8,128)}) %reduce-scatter.2.cloned.1.call-update) | async-done | bytes 1048592 | tf_op jit(solution)/shard_map/reduce_scatter | solution.py:174
  698.4 2.1 convert_element_type.67
  (45 shorter events, 0.3 us)
Async XLA Ops:
  6.5 59.2 %copy-start = (f32[256,32]{0,1:T(8,128)S(1)}, f32[256,32]{0,1:T(8,128)}, u32[]{:S(2)}) copy-start(f32[256,32]{0,1:T(8,128)} %param.20) | copy-start | bytes 98308
  6.5 691.9 %reduce-scatter.2.cloned.1.call-start = ((), (), s32[]{:S(2)}) async-start(), calls=%async_computation.1 | async-start | bytes 5242880 | tf_op jit(solution)/shard_map/reduce_scatter | solution.py:174
  6.5 48.8 %collective-permute-start.6 = (bf16[2048,512]{1,0:T(8,128)(2,1)}, bf16[2048,512]{1,0:T(8,128)(2,1)S(1)}, u32[]{:S(2)}, u32[]{:S(2)}) collective-permute-start(bf16[2048,512]{1,0:T(8,128)(2,1)} %param.23), channel_id=1, source_target_pairs={{0,4},{4,0},{8,12},{12,8},{16,20},{20,16},{24,28},{28,24},{1,5},{5... | collective-permute-start | bytes 6291464 | tf_op jit(solution)/shard_map/ppermute | solution.py:16
  9.5 52.6 %copy-start.3 = (bf16[256,2048]{1,0:T(8,128)(2,1)S(1)}, bf16[256,2048]{1,0:T(8,128)(2,1)}, u32[]{:S(2)}) copy-start(bf16[256,2048]{1,0:T(8,128)(2,1)} %param.12) | copy-start | bytes 3145732
  9.5 52.7 %copy-start.5 = (bf16[256,128]{1,0:T(8,128)(2,1)S(1)}, bf16[256,128]{1,0:T(8,128)(2,1)}, u32[]{:S(2)}) copy-start(bf16[256,128]{1,0:T(8,128)(2,1)} %param.13) | copy-start | bytes 196612
  9.5 52.7 %copy-start.6 = (bf16[256,128]{1,0:T(8,128)(2,1)S(1)}, bf16[256,128]{1,0:T(8,128)(2,1)}, u32[]{:S(2)}) copy-start(bf16[256,128]{1,0:T(8,128)(2,1)} %param.14) | copy-start | bytes 196612
  60.3 92.1 %collective-permute-start.7 = (bf16[2048,1024]{1,0:T(8,128)(2,1)}, bf16[2048,1024]{1,0:T(8,128)(2,1)}, u32[]{:S(2)}, u32[]{:S(2)}) collective-permute-start(bf16[2048,1024]{1,0:T(8,128)(2,1)} %maximum_select_fusion.3), channel_id=1, source_target_pairs={{0,8},{4,12},{8,0},{12,4},{16,24},{20,28},{24,16},{28,20},{1,9},{5... | collective-permute-start | bytes 12582920 | tf_op jit(solution)/shard_map/ppermute | solution.py:16
  62.3 105.1 %collective-permute-start = (bf16[3,2304]{1,0:T(4,128)(2,1)S(1)}, bf16[3,2304]{1,0:T(4,128)(2,1)S(1)}, u32[]{:S(2)}, u32[]{:S(2)}) collective-permute-start(bf16[3,2304]{1,0:T(4,128)(2,1)S(1)} %slice.83), channel_id=1, source_target_pairs={{0,4},{4,8},{8,12},{12,16},{16,20},{20,24},{24,28},{1,5},{5,9},{9,... | collective-permute-start | bytes 41480 | tf_op jit(solution)/shard_map/ppermute | solution.py:29
  66.5 99.7 %copy-start.8 = (f32[4,2048]{1,0:T(4,128)S(1)}, f32[4,2048]{1,0:T(4,128)}, u32[]{:S(2)}) copy-start(f32[4,2048]{1,0:T(4,128)} %param.16) | copy-start | bytes 98308
  66.5 99.7 %copy-start.9 = (f32[4,128]{1,0:T(4,128)S(1)}, f32[4,128]{1,0:T(4,128)}, u32[]{:S(2)}) copy-start(f32[4,128]{1,0:T(4,128)} %param.17) | copy-start | bytes 6148
  66.6 100.6 %copy-start.10 = (f32[4,128]{1,0:T(4,128)S(1)}, f32[4,128]{1,0:T(4,128)}, u32[]{:S(2)}) copy-start(f32[4,128]{1,0:T(4,128)} %param.18) | copy-start | bytes 6148
  163.6 450.7 %collective-permute-start.8 = (bf16[2048,2048]{1,0:T(8,128)(2,1)}, bf16[2048,2048]{1,0:T(8,128)(2,1)}, u32[]{:S(2)}, u32[]{:S(2)}) collective-permute-start(bf16[2048,2048]{1,0:T(8,128)(2,1)} %maximum_select_fusion.2), channel_id=1, source_target_pairs={{0,16},{4,20},{8,24},{12,28},{16,0},{20,4},{24,8},{28,12},{1,17},{... | collective-permute-start | bytes 25165832 | tf_op jit(solution)/shard_map/ppermute | solution.py:16
  170.6 2.0 copy-start.7
  174.0 23.8 %collective-permute-start.3 = (f32[1,32,64,128]{3,2,1,0:T(8,128)S(1)}, f32[1,32,64,128]{3,2,1,0:T(8,128)S(1)}, u32[]{:S(2)}, u32[]{:S(2)}) collective-permute-start(f32[1,32,64,128]{3,2,1,0:T(8,128)S(1)} %fusion.25), channel_id=1, source_target_pairs={{0,4},{4,8},{8,12},{12,16},{16,20},{20,24},{24,28},{1,5},{5,9},{9,... | collective-permute-start | bytes 3145736 | tf_op jit(solution)/shard_map/ppermute | solution.py:29
  197.9 1.0 copy-start.1
  200.1 357.8 %collective-permute-start.4 = (f32[1,32,64,128]{3,2,1,0:T(8,128)}, f32[1,32,64,128]{3,2,1,0:T(8,128)}, u32[]{:S(2)}, u32[]{:S(2)}) collective-permute-start(f32[1,32,64,128]{3,2,1,0:T(8,128)} %multiply_add_fusion.1), channel_id=1, source_target_pairs={{0,8},{4,12},{8,16},{12,20},{16,24},{20,28},{1,9},{5,13},{9,17},{1... | collective-permute-start | bytes 3145736 | tf_op jit(solution)/shard_map/ppermute | solution.py:29
  375.4 182.4 %collective-permute-start.1 = (f32[1,32]{1,0:T(1,128)S(1)}, f32[1,32]{1,0:T(1,128)S(1)}, u32[]{:S(2)}, u32[]{:S(2)}) collective-permute-start(f32[1,32]{1,0:T(1,128)S(1)} %bitcast.72), channel_id=1, source_target_pairs={{0,4},{4,8},{8,12},{12,16},{16,20},{20,24},{24,28},{1,5},{5,9},{9,... | collective-permute-start | bytes 392 | tf_op jit(solution)/shard_map/ppermute | solution.py:29
  559.6 48.6 %collective-permute-start.5 = (f32[1,32,64,128]{3,2,1,0:T(8,128)S(1)}, f32[1,32,64,128]{3,2,1,0:T(8,128)S(1)}, u32[]{:S(2)}, u32[]{:S(2)}) collective-permute-start(f32[1,32,64,128]{3,2,1,0:T(8,128)S(1)} %multiply_add_fusion), channel_id=1, source_target_pairs={{0,16},{4,20},{8,24},{12,28},{1,17},{5,21},{9,25},{13,29},{2,18},{... | collective-permute-start | bytes 3145736 | tf_op jit(solution)/shard_map/ppermute | solution.py:29
  584.1 21.7 %collective-permute-start.2 = (f32[1,32]{1,0:T(1,128)S(1)}, f32[1,32]{1,0:T(1,128)S(1)}, u32[]{:S(2)}, u32[]{:S(2)}) collective-permute-start(f32[1,32]{1,0:T(1,128)S(1)} %bitcast_multiply_fusion.1), channel_id=1, source_target_pairs={{0,8},{4,12},{8,16},{12,20},{16,24},{20,28},{1,9},{5,13},{9,17},{1... | collective-permute-start | bytes 392 | tf_op jit(solution)/shard_map/ppermute | solution.py:29
  606.0 2.1 copy-start.2
  606.0 2.1 copy-start.11
  611.5 2.0 copy-start.4
  613.5 0.8 copy-start.12
Sparse Core Ops, SparseCore 0:
  632.4 66.0 reduce-scatter.1
